TPU v7x, 32 devices: a whole 2x2x4 slice. The times are simulated.
32 devices in a mesh: row: 4 (over y, x), col: 8 (over z, core).
Axes of the slice: x: 2, y: 2, z: 4, core: 2. Of those that a mesh axis runs over, the one named last changes fastest.
Arguments:
- sensitivity: bfloat16 [8192, 8, 4096], P('row', None, 'col'), may hold values from -0.25 to 0.25
- sample_weight: float32 [8192], P('row'), may hold values from 0.2 to 5
- pattern: int32 [16, 8, 8], P('row', None, 'col'), may hold values 0 or 1
- prior: float32 [2048], P('row'), may hold values from 0.5 to 5
Outputs:
- factored_band: float32 [2048, 8, 4096], P('row', None, 'col')
Inputs may be any that keep to these rules, and one draw needn't show every extreme that they name: pattern holds only 0 and 1.
All inputs are finite; a program needn't handle non-finite values. No bound on the sum of `pattern` on one device may be relied on, other than what follows from the above.
Results may differ from a plain program's by a relative error of at most 0.0028.
Values may be sent and summed in bfloat16 or wider, within the bound.
No kernel may reach another device: no remote copies, remote signals or barrier semaphores. Data moves between devices by JAX's collectives and lax.ppermute only.
A program may use at most 128 MiB of HBM per device.

v0:
```python
import jax
import jax.numpy as jnp
from jax import lax
from jax.sharding import PartitionSpec as P


def spread(value, axis, root):
    mine = lax.axis_index(axis) == root
    return lax.psum(jnp.where(mine, value, jnp.zeros_like(value)), axis)


def body(sensitivity, sample_weight, pattern, prior):
    rows_here = sensitivity.shape[0]
    cycles = sensitivity.shape[1]
    tile = sensitivity.shape[2]
    blocks = pattern.shape[0]
    widths = cycles * tile
    mask_blocks = pattern.astype(jnp.bfloat16)[:, None, :, :]
    masked = (sensitivity.reshape(blocks, tile, cycles, tile) * mask_blocks).reshape(
        rows_here, widths
    )
    weighted = (sample_weight[:, None] * masked.astype(jnp.float32)).astype(jnp.bfloat16)
    first_tile = masked[:, :tile]
    row_count = lax.axis_size("row")
    band_parts = []
    for owner in range(row_count):
        band_parts.append(spread(first_tile, "col", owner))
    band = jnp.concatenate(band_parts, axis=1)
    band_weighted = (sample_weight[:, None] * band.astype(jnp.float32)).astype(jnp.bfloat16)
    head = lax.psum(
        jnp.einsum("sb,sc->bc", band[:, :tile], band_weighted, preferred_element_type=jnp.float32),
        "row",
    )
    prior_head = lax.all_gather(prior, "row", tiled=True)[:tile]
    identity = jnp.eye(tile, dtype=jnp.float32)
    corner = head[:, :tile] + identity * prior_head[None, :]
    lower = jnp.linalg.cholesky(corner)
    lower_inv = jax.scipy.linalg.solve_triangular(lower, identity, lower=True)
    hi = lax.Precision.HIGHEST
    side_panel = jnp.dot(lower_inv, head[:, tile:], precision=hi)
    side_t = jnp.dot(side_panel.T, lower_inv, precision=hi)
    transform = jnp.concatenate([lower_inv, -side_t], axis=0)
    part_head = jnp.einsum(
        "sb,sc->bc", band[:, :tile], weighted, preferred_element_type=jnp.float32
    )
    part_rest = jnp.einsum(
        "sb,sc->bc", band[:, tile:], weighted, preferred_element_type=jnp.float32
    )
    moved = jnp.dot(transform, part_head, precision=lax.Precision.HIGH)
    partial = moved + jnp.concatenate([jnp.zeros((tile, widths), jnp.float32), part_rest], axis=0)
    result = lax.psum_scatter(partial, "row", scatter_dimension=0, tiled=True)
    row = lax.axis_index("row")
    col = lax.axis_index("col")
    mine = lax.dynamic_slice_in_dim(transform, row * tile, tile, axis=0)
    head_on = (col == 0).astype(jnp.float32)
    diag_on = ((col == row) & (row != 0)).astype(jnp.float32)
    fix = head_on * mine * prior_head[None, :] + diag_on * identity * prior[None, :]
    result = result.at[:, :tile].add(fix)
    return result.reshape(tile, cycles, tile)


def solution(mesh):
    return jax.shard_map(
        body,
        mesh=mesh,
        in_specs=(P("row", None, "col"), P("row"), P("row", None, "col"), P("row")),
        out_specs=P("row", None, "col"),
        check_vma=False,
    )
```

profile of v0, /device:TPU:0, one launch (start us, length us, event | category | flops | bytes accessed | tf_op | source)
XLA Modules:
  0.0 846.0 jit_solution(15876469855539642256)
XLA Ops:
  6.5 0.7 convert_element_type.28
  7.2 1.7 mul.67
  9.0 6.3 copy.50
  15.2 12.2 %copy.49 = bf16[256,8,8,512]{3,1,2,0:T(8,128)(2,1)S(1)} copy(bf16[256,8,8,512]{3,2,1,0:T(8,128)(2,1)} %bitcast.65) | data formatting | bytes 33554432
  27.4 9.4 %mul.69 = bf16[2048,4096]{1,0:T(8,128)(2,1)} multiply(bf16[2048,4096]{1,0:T(8,128)(2,1)S(1)} %bitcast.63, bf16[2048,4096]{1,0:T(8,128)(2,1)S(1)} %bitcast.62) | non-fusion elementwise | flops 8388608 | bytes 50331648 | tf_op jit(solution)/shard_map/mul | solution.py:19
  36.8 5.1 broadcast_select_fusion.3
  41.9 0.6 copy-done.2
  42.5 9.6 %all-gather = f32[4,1,512]{2,1,0:T(1,128)S(1)} all-gather(f32[1,1,512]{2,1,0:T(1,128)S(1)} %bitcast.70), channel_id=1, replica_groups=mesh['row'=4,'col'=8] {'row'}, dimensions={0}, use_global_device_ids=true | all-gather | bytes 10240 | tf_op jit(solution)/shard_map/all_gather | solution.py:34
  52.3 168.0 %all-reduce.8.cloned.1.call-done = (bf16[2048,512]{1,0:T(8,128)(2,1)}, bf16[2048,512]{1,0:T(8,128)(2,1)}, bf16[2048,512]{1,0:T(8,128)(2,1)}, bf16[2048,512]{1,0:T(8,128)(2,1)}) async-done(((bf16[2048,512]{1,0:T(8,128)(2,1)}, bf16[2048,512]{1,0:T(8,128)(2,1)}, bf16[2048,512]{1,0:T(8,128)(2,1)}, bf16[2048,512]{1,0:T(8,128)(2,1)}), (bf16[2048,512]{1,0:T(8,128)(2,1)}, bf16[2048,512]{1,0:T(8,128)(2,1)}, ...) | async-done | bytes 8388624 | tf_op jit(solution)/shard_map/psum | solution.py:9
  220.3 12.8 %fusion = f32[512,2048]{0,1:T(8,128)} fusion(bf16[2048,512]{1,0:T(8,128)(2,1)} %get-tuple-element.44, bf16[2048,512]{1,0:T(8,128)(2,1)} %get-tuple-element.41, bf16[2048,512]{1,0:T(8,128)(2,1)} %get-tuple-element.42, bf16[2048,512]{1,0:T(8,128)(2,1)} %get-tuple-element.43, f32[2048]{0:T(1024)S(1)} %copy-done.4), kind=kOutput, calls=%fused_computation.5 | convolution fusion | flops 4336910336 | bytes 12591104 | tf_op jit(solution)/shard_map/sb,sc->bc/dot_general | solution.py:31
  233.2 0.5 reduce-scatter.2.cloned.1.call-start
  233.7 34.0 %fusion.9 = f32[1536,4096]{0,1:T(8,128)} fusion(bf16[2048,4096]{1,0:T(8,128)(2,1)} %mul.69, f32[2048]{0:T(1024)S(1)} %copy-done.4, bf16[2048,512]{1,0:T(8,128)(2,1)} %get-tuple-element.41, bf16[2048,512]{1,0:T(8,128)(2,1)} %get-tuple-element.42, bf16[2048,512]{1,0:T(8,128)(2,1)} %get-tuple-element.43), kind=kOutput, calls=%fused_computation.14 | convolution fusion | flops 25813843968 | bytes 48242688 | tf_op jit(solution)/shard_map/sb,sc->bc/dot_general | solution.py:46
  267.7 15.7 %fusion.10 = f32[512,4096]{1,0:T(8,128)} fusion(bf16[2048,512]{1,0:T(8,128)(2,1)S(1)} %copy-done.3, bf16[2048,4096]{1,0:T(8,128)(2,1)} %mul.69, f32[2048]{0:T(1024)S(1)} %copy-done.4), kind=kOutput, calls=%fused_computation.15 | convolution fusion | flops 8615100416 | bytes 27271168 | tf_op jit(solution)/shard_map/sb,sc->bc/dot_general | solution.py:43
  283.5 53.6 %all-reduce.6.cloned.1.call-done = f32[512,2048]{0,1:T(8,128)} async-done(((f32[512,2048]{0,1:T(8,128)}), f32[512,2048]{0,1:T(8,128)}) %all-reduce.6.cloned.1.call-update) | async-done | bytes 4194320 | tf_op jit(solution)/shard_map/psum | solution.py:30
  337.1 1.4 slice_add_fusion
  338.4 0.3 copy.24
  338.8 1.5 fusion.20
  340.3 11.7 %cholesky.103 = f32[128,128]{1,0:T(8,128)S(1)} custom-call(f32[128,128]{1,0:T(8,128)S(1)} %cholesky.263), custom_call_target="Cholesky" | custom-call | tf_op jit(solution)/shard_map/jit(cholesky)/cholesky | solution.py:37
  352.0 9.8 %custom-call.31 = f32[1,128,128]{1,2,0:T(8,128)S(1)} custom-call(f32[1,128,128]{2,1,0:T(8,128)S(1)} %get-tuple-element.56), custom_call_target="InvertDiagBlocksLowerTriangular" | custom-call | tf_op jit(solution)/shard_map/jit(cholesky)/cholesky | solution.py:37
  361.8 0.3 fusion.35
  362.2 0.3 convolution_subtract_fusion.3
  362.5 11.7 %cholesky.215 = f32[128,128]{1,0:T(8,128)S(1)} custom-call(f32[128,128]{1,0:T(8,128)S(1)} %cholesky.267), custom_call_target="Cholesky" | custom-call | tf_op jit(solution)/shard_map/jit(cholesky)/cholesky | solution.py:37
  374.6 10.2 %custom-call.32 = f32[1,128,128]{1,2,0:T(8,128)S(1)} custom-call(f32[1,128,128]{2,1,0:T(8,128)S(1)} %get-tuple-element.54), custom_call_target="InvertDiagBlocksLowerTriangular" | custom-call | tf_op jit(solution)/shard_map/jit(cholesky)/cholesky | solution.py:37
  385.0 0.3 convolution_dynamic-update-slice_fusion
  385.3 1.5 convolution_subtract_fusion.4
  386.8 11.7 %cholesky.236 = f32[128,128]{1,0:T(8,128)S(1)} custom-call(f32[128,128]{1,0:T(8,128)S(1)} %cholesky.272), custom_call_target="Cholesky" | custom-call | tf_op jit(solution)/shard_map/jit(cholesky)/cholesky | solution.py:37
  398.7 9.8 %custom-call.33 = f32[1,128,128]{1,2,0:T(8,128)S(1)} custom-call(f32[1,128,128]{2,1,0:T(8,128)S(1)} %get-tuple-element.52), custom_call_target="InvertDiagBlocksLowerTriangular" | custom-call | tf_op jit(solution)/shard_map/jit(cholesky)/cholesky | solution.py:37
  408.8 1.3 convolution_subtract_fusion.5
  410.1 11.9 %cholesky.253 = f32[128,128]{1,0:T(8,128)S(1)} custom-call(f32[128,128]{1,0:T(8,128)S(1)} %convolution_subtract_fusion.5), custom_call_target="Cholesky" | custom-call | tf_op jit(solution)/shard_map/jit(cholesky)/cholesky | solution.py:37
  422.1 0.7 compare_reduce_fusion.2
  422.8 0.6 compare_reduce_fusion.1
  423.4 0.7 compare_reduce_fusion.3
  426.7 10.7 %while.2 = (s32[]{:T(128)}, f32[512,512]{0,1:T(8,128)S(1)}, s32[4,2]{0,1:T(2,128)S(1)}, f32[4,128,128]{2,1,0:T(8,128)}, s32[]{:T(128)}) while((s32[]{:T(128)}, f32[512,512]{0,1:T(8,128)S(1)}, s32[4,2]{0,1:T(2,128)S(1)}, f32[4,128,128]{2,1,0:T(8,128)}, s32[]{:T(128)}) %tuple.32), condition=%wide.while_cond.1, body=%wide.while_body.1.sunk | while | flops 2 | bytes 393829 | solution.py:38
  426.8 0.6 fusion.67
  427.4 1.3 dynamic-slice.15
  428.8 0.6 bitcast_dynamic-update-slice_fusion.2
  429.5 0.6 fusion.67
  430.1 1.3 dynamic-slice.15
  431.5 0.6 bitcast_dynamic-update-slice_fusion.2
  432.2 0.6 fusion.67
  432.7 1.3 dynamic-slice.15
  434.1 0.6 bitcast_dynamic-update-slice_fusion.2
  434.8 0.6 fusion.67
  435.4 1.3 dynamic-slice.15
  436.8 0.6 bitcast_dynamic-update-slice_fusion.2
  437.4 40.1 %custom-call.34 = f32[4,128,128]{1,2,0:T(8,128)S(1)} custom-call(f32[4,128,128]{2,1,0:T(8,128)} %get-tuple-element.24), custom_call_target="InvertDiagBlocksLowerTriangular" | custom-call | tf_op jit(solution)/shard_map/jit(_solve_triangular)/triangular_solve | solution.py:38
  477.6 0.3 fusion.31
  477.9 0.6 convolution_subtract_fusion.1
  478.5 0.4 fusion.43
  478.9 1.0 convolution_subtract_fusion
  479.9 1.3 fusion.41
  481.2 1.5 convolution_subtract_fusion.2
  483.1 1.3 fusion.40
  484.5 0.8 constant_dynamic-update-slice_fusion.3
  485.2 0.7 constant_dynamic-update-slice_fusion.2
  486.0 0.7 constant_dynamic-update-slice_fusion.1
  486.7 0.8 constant_dynamic-update-slice_fusion
  487.5 7.3 fusion.17
  494.8 7.2 fusion.16
  502.0 34.8 %pad_add_fusion = f32[2048,4096]{0,1:T(8,128)} fusion(f32[1536,4096]{0,1:T(8,128)} %fusion.9, f32[2048,512]{0,1:T(8,128)} %fusion.16, f32[512,4096]{1,0:T(8,128)} %fusion.10), kind=kOutput, calls=%fused_computation.2 | convolution fusion | flops 25778192384 | bytes 71303168 | tf_op jit(solution)/shard_map/dot_general | solution.py:49
  536.8 0.6 compare_reduce_fusion
  537.4 288.0 %reduce-scatter.2.cloned.1.call-done = f32[512,4096]{0,1:T(8,128)} async-done(((f32[2048,4096]{0,1:T(8,128)}), f32[512,4096]{0,1:T(8,128)}) %reduce-scatter.2.cloned.1.call-update) | async-done | bytes 8388624 | tf_op jit(solution)/shard_map/reduce_scatter | solution.py:51
  825.4 3.4 fusion.19
  828.9 10.4 %copy.40 = f32[512,8,512]{2,1,0:T(8,128)} copy(f32[512,8,512]{0,2,1:T(8,128)} %bitcast.66) | data formatting | bytes 16777216 | tf_op jit(solution)/shard_map/reshape | solution.py:59
  (52 shorter events, 2.7 us)
Async XLA Ops:
  6.5 213.8 %all-reduce.8.cloned.1.call-start = ((), (), s32[]{:S(2)}) async-start(), calls=%async_computation.3 | async-start | bytes 16777216 | tf_op jit(solution)/shard_map/psum | solution.py:9
  41.8 0.7 copy-start.2
  41.8 178.5 %copy-start.4 = (f32[2048]{0:T(1024)S(1)}, f32[2048]{0:T(1024)}, u32[]{:S(2)}) copy-start(f32[2048]{0:T(1024)} %param.7) | copy-start | bytes 24580
  41.9 295.2 %all-reduce.6.cloned.1.call-start = ((), (), s32[]{:S(2)}) async-start(), calls=%async_computation.1 | async-start | bytes 8388608 | tf_op jit(solution)/shard_map/psum | solution.py:30
  233.2 34.6 %copy-start.3 = (bf16[2048,512]{1,0:T(8,128)(2,1)S(1)}, bf16[2048,512]{1,0:T(8,128)(2,1)}, u32[]{:S(2)}) copy-start(bf16[2048,512]{1,0:T(8,128)(2,1)} %get-tuple-element.44) | copy-start | bytes 6291460
  233.2 592.3 %reduce-scatter.2.cloned.1.call-start = ((), (), s32[]{:S(2)}) async-start(), calls=%async_computation.2 | async-start | bytes 41943040 | tf_op jit(solution)/shard_map/reduce_scatter | solution.py:51
  340.3 34.4 %copy-start = (f32[512,512]{1,0:T(8,128)}, f32[512,512]{1,0:T(8,128)S(1)}, u32[]{:S(2)}) copy-start(f32[512,512]{1,0:T(8,128)S(1)} %fusion.20) | copy-start | bytes 3145732
  477.6 0.9 copy-start.1
Sparse Core Ops, SparseCore 0:
  42.0 178.3 all-reduce.7
  233.3 103.7 all-reduce.5
  536.9 288.5 reduce-scatter.1
where the time goes:
time: 853 us; the launch traced here: 846 us
  waiting for transfers between devices  510 us (60%)
  other arithmetic  141 us (17%)
  matrix products  122 us (14%)
  local copies, waits for them, and re-layouts  46.3 us (5%)
  between operations  16.2 us (2%)
  blocking collectives  9.56 us (1%)
    reduce_scatter x1, waiting for transfers between devices, body(): result = lax.psum_scatter(partial, 'row', scatter_dimension=0, tiled=True)  288 us
    psum x1, waiting for transfers between devices, spread(): return lax.psum(jnp.where(mine, value, jnp.zeros_like(value)), axis)  168 us
    another operation x14, other arithmetic, body(): lower = jnp.linalg.cholesky(corner)  78.9 us
    psum x1, waiting for transfers between devices, body(): lax.psum(jnp.einsum('sb,sc->bc', band[:, :tile], band_weighted, preferred...  53.6 us
    another operation x3, other arithmetic, body(): lower_inv = jax.scipy.linalg.solve_triangular(lower, identity, lower=True)  40.3 us
    dot_general x1, matrix products, body(): moved = jnp.dot(transform, part_head, precision=lax.Precision.HIGH)  34.8 us
    dot_general x1, matrix products, body(): jnp.einsum('sb,sc->bc', band[:, tile:], weighted, preferred_element_type=...  34 us
    unnamed x17, local copies, waits for them, and re-layouts  22 us
  transfers between devices with their start and end apart: 3, of which 3 were waited for; matrix products, arithmetic and copies ran while one was open for 6% of the time, Pallas kernels for 0%

commit v1 on v0

--- a/solution.py
+++ b/solution.py
@@ -6,7 +6,7 @@
 
 def spread(value, axis, root):
     mine = lax.axis_index(axis) == root
-    return lax.psum(jnp.where(mine, value, jnp.zeros_like(value)), axis)
+    return jnp.sum(lax.all_gather(jnp.where(mine, value, jnp.zeros_like(value)), axis), axis=0)
 
 
 def body(sensitivity, sample_weight, pattern, prior):

time: 853 us -> 1290 us (1.51)
  waiting for transfers between devices: 510 us -> 905 us
  other arithmetic: 141 us -> 183 us
    all_gather x0 -> x4, waiting for transfers between devices: none -> 563 us  [spread(): lax.all_gather(jnp.where(mine, value, jnp.zeros_like(value)), axis)]
    psum x1 -> x0, waiting for transfers between devices: 168 us -> none  [spread(): return lax.psum(jnp.where(mine, value, jnp.zeros_like(value)), axis)]
    reduce_sum x0 -> x4, other arithmetic: none -> 42 us  [spread(): jnp.sum(lax.all_gather(jnp.where(mine, value, jnp.zeros_like(value)), axi...]
  transfers between devices with their start and end apart: 3 -> 6, of which waited for: 3 -> 6; matrix products, arithmetic and copies ran while one was open for 6% -> 6% of each run, Pallas kernels for 0% -> 0%
where the time goes in v1:
time: 1290 us; the launch traced here: 1280 us
  waiting for transfers between devices  905 us (70%)
  other arithmetic  183 us (14%)
  matrix products  120 us (9%)
  local copies, waits for them, and re-layouts  45.7 us (4%)
  between operations  16.7 us (1%)
    all_gather x4, waiting for transfers between devices, spread(): lax.all_gather(jnp.where(mine, value, jnp.zeros_like(value)), axis)  563 us
    reduce_scatter x1, waiting for transfers between devices, body(): result = lax.psum_scatter(partial, 'row', scatter_dimension=0, tiled=True)  288 us
    another operation x14, other arithmetic, body(): lower = jnp.linalg.cholesky(corner)  78.9 us
    psum x1, waiting for transfers between devices, body(): lax.psum(jnp.einsum('sb,sc->bc', band[:, :tile], band_weighted, preferred...  51.5 us
    reduce_sum x4, other arithmetic, spread(): jnp.sum(lax.all_gather(jnp.where(mine, value, jnp.zeros_like(value)), axi...  42 us
    another operation x3, other arithmetic, body(): lower_inv = jax.scipy.linalg.solve_triangular(lower, identity, lower=True)  40.3 us
    dot_general x1, matrix products, body(): jnp.einsum('sb,sc->bc', band[:, tile:], weighted, preferred_element_type=...  34.8 us
    dot_general x1, matrix products, body(): moved = jnp.dot(transform, part_head, precision=lax.Precision.HIGH)  34.8 us
  transfers between devices with their start and end apart: 6, of which 6 were waited for; matrix products, arithmetic and copies ran while one was open for 6% of the time, Pallas kernels for 0%

profile of v1, /device:TPU:0, one launch (start us, length us, event | category | flops | bytes accessed | tf_op | source)
XLA Modules:
  0.0 1280.9 jit_solution(15716190443234742049)
XLA Ops:
  6.5 0.7 convert_element_type.36
  7.2 1.7 mul.67
  9.0 6.3 copy.50
  15.2 12.2 copy.49
  27.4 9.4 mul.69
  36.8 5.1 broadcast_select_fusion.3
  41.9 0.7 all-gather.12.cloned.1.call-update
  42.7 0.7 all-gather.14.cloned.1.call-update
  44.0 9.6 all-gather.4
  53.8 142.0 %all-gather.10.cloned.1.call-done = bf16[16384,512]{1,0:T(8,128)(2,1)} async-done(((bf16[2048,512]{1,0:T(8,128)(2,1)}), bf16[16384,512]{1,0:T(8,128)(2,1)}) %all-gather.10.cloned.1.call-update) | async-done | bytes 16777232 | tf_op jit(solution)/shard_map/all_gather | solution.py:9
  195.8 9.6 reduce_sum.48
  205.4 141.3 %all-gather.12.cloned.1.call-done = bf16[16384,512]{1,0:T(8,128)(2,1)} async-done(((bf16[2048,512]{1,0:T(8,128)(2,1)}), bf16[16384,512]{1,0:T(8,128)(2,1)}) %all-gather.12.cloned.1.call-update) | async-done | bytes 16777232 | tf_op jit(solution)/shard_map/all_gather | solution.py:9
  346.7 10.9 reduce_sum.49
  357.6 140.0 %all-gather.14.cloned.1.call-done = bf16[16384,512]{1,0:T(8,128)(2,1)} async-done(((bf16[2048,512]{1,0:T(8,128)(2,1)}), bf16[16384,512]{1,0:T(8,128)(2,1)}) %all-gather.14.cloned.1.call-update) | async-done | bytes 16777232 | tf_op jit(solution)/shard_map/all_gather | solution.py:9
  497.6 11.0 reduce_sum.50
  508.6 139.7 %all-gather.16.cloned.1.call-done = bf16[16384,512]{1,0:T(8,128)(2,1)} async-done(((bf16[2048,512]{1,0:T(8,128)(2,1)}), bf16[16384,512]{1,0:T(8,128)(2,1)}) %all-gather.16.cloned.1.call-update) | async-done | bytes 16777232 | tf_op jit(solution)/shard_map/all_gather | solution.py:9
  648.4 10.5 reduce_sum.51
  658.9 10.6 fusion
  670.0 34.8 %fusion.9 = f32[1536,4096]{0,1:T(8,128)} fusion(bf16[2048,4096]{1,0:T(8,128)(2,1)} %mul.69, f32[2048]{0:T(1024)S(1)} %copy-done.3, bf16[2048,512]{1,0:T(8,128)(2,1)} %reduce_sum.51, bf16[2048,512]{1,0:T(8,128)(2,1)} %reduce_sum.50, bf16[2048,512]{1,0:T(8,128)(2,1)} %reduce_sum.49), kind=kOutput, calls=%fused_computation.14 | convolution fusion | flops 25813843968 | bytes 48242688 | tf_op jit(solution)/shard_map/sb,sc->bc/dot_general | solution.py:46
  704.8 15.1 %fusion.10 = f32[512,4096]{1,0:T(8,128)} fusion(bf16[2048,512]{1,0:T(8,128)(2,1)S(1)} %reduce_sum.48, bf16[2048,4096]{1,0:T(8,128)(2,1)} %mul.69, f32[2048]{0:T(1024)S(1)} %copy-done.3), kind=kOutput, calls=%fused_computation.15 | convolution fusion | flops 8615100416 | bytes 27271168 | tf_op jit(solution)/shard_map/sb,sc->bc/dot_general | solution.py:43
  719.9 51.5 %all-reduce.4.cloned.1.call-done = f32[512,2048]{0,1:T(8,128)} async-done(((f32[512,2048]{0,1:T(8,128)}), f32[512,2048]{0,1:T(8,128)}) %all-reduce.4.cloned.1.call-update) | async-done | bytes 4194320 | tf_op jit(solution)/shard_map/psum | solution.py:30
  771.5 1.4 slice_add_fusion
  773.2 1.5 fusion.20
  774.7 11.7 cholesky.103
  786.5 9.8 custom-call.31
  796.9 11.7 cholesky.215
  809.0 10.2 custom-call.32
  819.7 1.5 convolution_subtract_fusion.4
  821.2 11.7 cholesky.236
  833.1 9.8 custom-call.33
  843.2 1.3 convolution_subtract_fusion.5
  844.5 11.9 cholesky.253
  856.5 0.7 compare_reduce_fusion.2
  857.2 0.6 compare_reduce_fusion.1
  857.8 0.7 compare_reduce_fusion.3
  861.2 10.7 while.2
  861.3 0.6 fusion.67
  861.8 1.3 dynamic-slice.15
  863.2 0.6 bitcast_dynamic-update-slice_fusion.2
  863.9 0.6 fusion.67
  864.5 1.3 dynamic-slice.15
  865.9 0.6 bitcast_dynamic-update-slice_fusion.2
  866.6 0.6 fusion.67
  867.1 1.3 dynamic-slice.15
  868.6 0.6 bitcast_dynamic-update-slice_fusion.2
  869.8 1.3 dynamic-slice.15
  871.2 0.6 bitcast_dynamic-update-slice_fusion.2
  871.9 40.1 %custom-call.34 = f32[4,128,128]{1,2,0:T(8,128)S(1)} custom-call(f32[4,128,128]{2,1,0:T(8,128)} %get-tuple-element.24), custom_call_target="InvertDiagBlocksLowerTriangular" | custom-call | tf_op jit(solution)/shard_map/jit(_solve_triangular)/triangular_solve | solution.py:38
  912.3 0.6 convolution_subtract_fusion.1
  913.3 1.0 convolution_subtract_fusion
  914.3 1.3 fusion.41
  915.6 1.5 convolution_subtract_fusion.2
  917.5 1.3 fusion.40
  918.9 0.8 constant_dynamic-update-slice_fusion.3
  919.7 0.7 constant_dynamic-update-slice_fusion.2
  920.4 0.7 constant_dynamic-update-slice_fusion.1
  921.1 0.8 constant_dynamic-update-slice_fusion
  921.9 7.3 fusion.17
  929.2 7.2 fusion.16
  936.4 34.8 %pad_add_fusion = f32[2048,4096]{0,1:T(8,128)} fusion(f32[1536,4096]{0,1:T(8,128)} %fusion.9, f32[2048,512]{0,1:T(8,128)} %fusion.16, f32[512,4096]{1,0:T(8,128)} %fusion.10), kind=kOutput, calls=%fused_computation.2 | convolution fusion | flops 25778192384 | bytes 71303168 | tf_op jit(solution)/shard_map/dot_general | solution.py:49
  971.2 0.6 compare_reduce_fusion
  971.8 288.0 %reduce-scatter.2.cloned.1.call-done = f32[512,4096]{0,1:T(8,128)} async-done(((f32[2048,4096]{0,1:T(8,128)}), f32[512,4096]{0,1:T(8,128)}) %reduce-scatter.2.cloned.1.call-update) | async-done | bytes 8388624 | tf_op jit(solution)/shard_map/reduce_scatter | solution.py:51
  1259.9 3.4 fusion.19
  1263.3 10.4 copy.40
  (63 shorter events, 6.4 us)
Async XLA Ops:
  6.5 189.3 %all-gather.10.cloned.1.call-start = ((), (), s32[]{:S(2)}) async-start(), calls=%async_computation.3 | async-start | bytes 18874368 | tf_op jit(solution)/shard_map/all_gather | solution.py:9
  41.8 2.1 copy-start.2
  41.9 304.9 %all-gather.12.cloned.1.call-start = ((), (), s32[]{:S(2)}) async-start(), calls=%async_computation.4 | async-start | bytes 18874368 | tf_op jit(solution)/shard_map/all_gather | solution.py:9
  42.6 455.0 %all-gather.14.cloned.1.call-start = ((), (), s32[]{:S(2)}) async-start(), calls=%async_computation.5 | async-start | bytes 18874368 | tf_op jit(solution)/shard_map/all_gather | solution.py:9
  43.3 605.0 %all-gather.16.cloned.1.call-start = ((), (), s32[]{:S(2)}) async-start(), calls=%async_computation.6 | async-start | bytes 18874368 | tf_op jit(solution)/shard_map/all_gather | solution.py:9
  43.9 727.6 %all-reduce.4.cloned.1.call-start = ((), (), s32[]{:S(2)}) async-start(), calls=%async_computation.1 | async-start | bytes 8388608 | tf_op jit(solution)/shard_map/psum | solution.py:30
  648.4 10.5 copy-start.3
  669.5 590.3 %reduce-scatter.2.cloned.1.call-start = ((), (), s32[]{:S(2)}) async-start(), calls=%async_computation.2 | async-start | bytes 41943040 | tf_op jit(solution)/shard_map/reduce_scatter | solution.py:51
  774.7 34.4 %copy-start = (f32[512,512]{1,0:T(8,128)}, f32[512,512]{1,0:T(8,128)S(1)}, u32[]{:S(2)}) copy-start(f32[512,512]{1,0:T(8,128)S(1)} %fusion.20) | copy-start | bytes 3145732
  912.0 0.9 copy-start.1
Sparse Core Ops, SparseCore 0:
  42.0 153.7 all-gather.9
  197.4 149.2 all-gather.11
  348.3 149.2 all-gather.13
  499.1 149.2 all-gather.15
  669.6 101.7 all-reduce.3
  971.3 288.5 reduce-scatter.1
